TPU v7x, 512 devices: a whole 4x8x8 slice. The times are simulated.
512 devices in a mesh: req: 64 (over x, z, core), mdl: 8 (over y).
Axes of the slice: x: 4, y: 8, z: 8, core: 2. Of those that a mesh axis runs over, the one named last changes fastest.
Arguments:
- queries: bfloat16 [1536, 2048], P('req', 'mdl'), may hold values from -6 to 6
- scored_key_value: bfloat16 [2, 1536, 1024], P(None, 'req', 'mdl'), may hold values from -6 to 6
- gate_logits: bfloat16 [1536, 2048], P('req', 'mdl'), may hold values from -8 to 8
- page_kv: bfloat16 [2, 2176, 128, 1024], P(None, 'req', None, 'mdl'), may hold values from -6 to 6
- page_table: int32 [64, 128], replicated, may hold values from -1 to 2175, as said below
- lengths: int32 [64], replicated, may hold values from 1 to 16384
- assignment: int32 [64], replicated, may hold values from 0 to 63, each once
- offsets: int32 [64, 24], P('req'), may hold values from 0 to 23, each once within a row
- residual: bfloat16 [1536, 2048], P('req'), may hold values from -18 to 18
- out_weight: bfloat16 [2048, 2048], P('mdl'), may hold values from -1 to 1
- norm_gain: bfloat16 [2048], replicated, may hold values from 0.5 to 1.5
- head_weight: bfloat16 [2048, 131072], P(None, ('req', 'mdl')), may hold values from -0.3193592 to 0.3193592
- targets: int32 [1536], replicated, may hold values from 0 to 131071
Outputs:
- logprob: float32 [1536], P('req')
- entropy: float32 [1536], P('req')
Inputs may be any that keep to these rules, and one draw needn't show every extreme that they name: `page_table`: row i lists the pages of request i in order, each as owner index times 34 plus a slot, followed by -1. Request i has ceil(lengths[i] / 128) pages, no page serves two requests, and at most 2 pages of one request sit on one owner. `assignment`: each index along req holds exactly one request. `offsets`: each row is an order of 0 to 23.
All inputs are finite; a program needn't handle non-finite values.
Results may differ from a plain program's by a relative error of at most 0.0013.
Values may be sent and summed in bfloat16 or wider, within the bound.
No kernel may reach another device: no remote copies, remote signals or barrier semaphores. Data moves between devices by JAX's collectives and lax.ppermute only.
A program may use at most 128 MiB of HBM per device.

v0:
```python
import jax
import jax.numpy as jnp
from jax import lax
from jax.sharding import PartitionSpec as P

HEAD_SIZE = 128
CAP = 2
FLOOR_SCORE = -1e30
NORM_EPSILON = 1e-06


def merge_stats(parts):
    peak = jnp.max(parts[:, :, 0], axis=0)
    scale = jnp.exp(parts[:, :, 0] - peak[None])
    total = jnp.sum(parts[:, :, 1] * scale, axis=0)
    moment = jnp.sum(parts[:, :, 2] * scale, axis=0)
    chosen = jnp.sum(parts[:, :, 3], axis=0)
    return jnp.stack([peak, total, moment, chosen], axis=1)


def body(
    queries,
    scored_key_value,
    gate_logits,
    page_kv,
    page_table,
    lengths,
    assignment,
    offsets,
    residual,
    out_weight,
    norm_gain,
    head_weight,
    targets,
):
    groups = lax.axis_size("req")
    req_index = lax.axis_index("req")
    fresh_count = queries.shape[0]
    kv_heads = scored_key_value.shape[2] // HEAD_SIZE
    queries_per_group = queries.shape[1] // scored_key_value.shape[2]
    page_len = page_kv.shape[2]
    store_pages = page_kv.shape[1]
    page_slots = page_table.shape[1]
    score_scale = HEAD_SIZE ** (-0.5)
    indices = jnp.arange(groups, dtype=jnp.int32)
    holder = jnp.sum(
        jnp.where(assignment[:, None] == indices[None, :], indices[:, None], 0), axis=0
    )
    query_heads = queries.reshape(fresh_count, kv_heads, queries_per_group, HEAD_SIZE)
    scored_keys = scored_key_value[0].reshape(fresh_count, kv_heads, HEAD_SIZE)
    scored_values = scored_key_value[1].reshape(fresh_count, kv_heads, HEAD_SIZE)
    fresh_order = offsets[0]
    visible = fresh_order[None, :] <= fresh_order[:, None]
    fresh_scores = (
        jnp.einsum("tjgd,ujd->jgtu", query_heads, scored_keys, preferred_element_type=jnp.float32)
        * score_scale
    )
    fresh_scores = jnp.where(visible[None, None], fresh_scores, FLOOR_SCORE)
    fresh_top = jnp.max(fresh_scores, axis=-1)
    page_owner = jnp.where(page_table >= 0, page_table // store_pages, -1)
    page_slot = page_table % store_pages
    is_mine = page_owner == req_index
    page_rank = jnp.cumsum(is_mine.astype(jnp.int32), axis=1) - 1
    slot_picks = [
        jnp.sum(jnp.where(is_mine & (page_rank == cap_index), page_slot, 0), axis=1)
        for cap_index in range(CAP)
    ]
    send_slot = jnp.take(jnp.stack(slot_picks, axis=1), holder, axis=0).reshape(-1)
    outgoing = jnp.take(page_kv, send_slot, axis=1)
    arrived = lax.all_to_all(outgoing, "req", split_axis=1, concat_axis=1, tiled=True)
    request = holder[req_index]
    page_table_row = jnp.take(page_table, request, axis=0)
    length = jnp.take(lengths, request)
    row_owner = jnp.where(page_table_row >= 0, page_table_row // store_pages, -1)
    source = row_owner[None, :] == indices[:, None]
    row_rank = jnp.cumsum(source.astype(jnp.int32), axis=1) - 1
    page_fill = jnp.clip(length - jnp.arange(page_slots, dtype=jnp.int32) * page_len, 0, page_len)
    counts = jnp.stack(
        [
            jnp.sum(jnp.where(source & (row_rank == cap_index), page_fill[None, :], 0), axis=1)
            for cap_index in range(CAP)
        ],
        axis=1,
    ).reshape(-1)
    live_keys = (jnp.arange(page_len, dtype=jnp.int32)[None, :] < counts[:, None]).reshape(-1)
    cached_keys = arrived[0].reshape(-1, kv_heads, HEAD_SIZE)
    cached_values = arrived[1].reshape(-1, kv_heads, HEAD_SIZE)
    scores = (
        jnp.einsum("tjgd,ljd->jgtl", query_heads, cached_keys, preferred_element_type=jnp.float32)
        * score_scale
    )
    scores = jnp.where(live_keys[None, None, None, :], scores, FLOOR_SCORE)
    row_top = jnp.maximum(jnp.max(scores, axis=-1), fresh_top)
    weights = jnp.exp(scores - row_top[..., None])
    weight_sum = jnp.sum(weights, axis=-1)
    summed = jnp.einsum(
        "jgtl,ljd->tjgd",
        weights.astype(jnp.bfloat16),
        cached_values,
        preferred_element_type=jnp.float32,
    )
    fresh_weights = jnp.exp(fresh_scores - row_top[..., None])
    weight_sum = weight_sum + jnp.sum(fresh_weights, axis=-1)
    summed = summed + jnp.einsum(
        "jgtu,ujd->tjgd",
        fresh_weights.astype(jnp.bfloat16),
        scored_values,
        preferred_element_type=jnp.float32,
    )
    attended = summed / jnp.transpose(weight_sum, (2, 0, 1))[..., None]
    gated_out = (
        attended.reshape(fresh_count, -1) * jax.nn.sigmoid(gate_logits.astype(jnp.float32))
    ).astype(jnp.bfloat16)
    update = lax.psum(jnp.dot(gated_out, out_weight, preferred_element_type=jnp.float32), "mdl")
    stream = residual.astype(jnp.float32) + update
    normed = (
        stream
        * lax.rsqrt(jnp.mean(stream * stream, axis=-1, keepdims=True) + NORM_EPSILON)
        * norm_gain.astype(jnp.float32)
    ).astype(jnp.bfloat16)
    logits = jnp.dot(
        lax.all_gather(normed, "req", axis=0, tiled=True),
        head_weight,
        preferred_element_type=jnp.float32,
    )
    vocab_width = head_weight.shape[1]
    mdl_size = lax.axis_size("mdl")
    mdl_index = lax.axis_index("mdl")
    vocab_start = (req_index * mdl_size + mdl_index) * vocab_width
    columns = vocab_start + jnp.arange(vocab_width, dtype=jnp.int32)
    chosen = jnp.sum(jnp.where(targets[:, None] == columns[None, :], logits, 0.0), axis=1)
    local_peak = jnp.max(logits, axis=1)
    local_weights = jnp.exp(logits - local_peak[:, None])
    stats = jnp.stack(
        [
            local_peak,
            jnp.sum(local_weights, axis=1),
            jnp.sum(local_weights * logits, axis=1),
            chosen,
        ],
        axis=1,
    ).reshape(groups, fresh_count, 4)
    stats = lax.all_to_all(stats, "req", 0, 0, tiled=True)
    stats = merge_stats(stats)
    slots = jnp.where(
        (jnp.arange(mdl_size, dtype=jnp.int32) == mdl_index)[:, None, None], stats[None], 0.0
    )
    stats = merge_stats(lax.psum(slots, "mdl"))
    row_peak, vocab_total, moment, chosen = (stats[:, i] for i in range(4))
    log_total = row_peak + jnp.log(vocab_total)
    logprob = chosen - log_total
    entropy = log_total - moment / vocab_total
    return (logprob, entropy)


def solution(mesh):
    placed = (
        P("req", "mdl"),
        P(None, "req", "mdl"),
        P("req", "mdl"),
        P(None, "req", None, "mdl"),
        P(),
        P(),
        P(),
        P("req", None),
        P("req", None),
        P("mdl", None),
        P(),
        P(None, ("req", "mdl")),
        P(),
    )
    return jax.shard_map(
        body, mesh=mesh, in_specs=placed, out_specs=(P("req"), P("req")), check_vma=False
    )
```

profile of v0, /device:TPU:2, one launch (start us, length us, event | category | flops | bytes accessed | tf_op | source)
XLA Modules:
  0.0 460.2 jit_solution(17138256541954221748)
XLA Ops:
  7.2 0.9 select_reduce_fusion.5
  8.1 0.8 fusion.57
  8.9 0.3 reduce_window_sum.17
  9.2 0.9 select_reduce_fusion.4
  10.1 0.1 copy.49
  10.2 0.6 gather_fusion
  10.8 0.1 broadcast_select_fusion
  10.9 0.1 select_n.156
  11.1 0.1 select_n.154
  11.2 6.4 %gather_fusion.1 = bf16[128,2,128,128]{3,2,1,0:T(8,128)(2,1)} fusion(bf16[2,34,128,128]{3,2,1,0:T(8,128)(2,1)S(1)} %copy-done, s32[1024]{0:T(1024)S(1)} %pad_clamp_fusion), kind=kCustom, calls=%fused_computation.1 | custom fusion | bytes 16777728 | tf_op jit(solution)/shard_map/jit(_take)/gather | solution.py:69
  17.6 7.4 %select_bitcast_fusion = bf16[2,128,128,128]{3,2,0,1:T(8,128)(2,1)} fusion(bf16[128,2,128,128]{3,2,1,0:T(8,128)(2,1)} %gather_fusion.1, pred[128]{0:T(512)(128)(4,1)S(1)} %compare_and_fusion), kind=kLoop, calls=%fused_computation.6 | loop fusion | flops 4194304 | bytes 16777344 | tf_op jit(solution)/shard_map/jit(_take)/select_n | solution.py:69
  25.0 14.2 %all-to-all-start = ((bf16[2,128,128,128]{3,2,0,1:T(8,128)(2,1)}), bf16[2,128,128,128]{3,2,0,1:T(8,128)(2,1)}, u32[]{:S(2)}, u32[]{:S(2)}) async-start(bf16[2,128,128,128]{3,2,0,1:T(8,128)(2,1)} %select_bitcast_fusion), calls=%async_computation | async-start | bytes 16777216 | tf_op jit(solution)/shard_map/all_to_all | solution.py:70
  39.3 0.6 dynamic_slice.3
  41.8 0.6 dynamic-slice.6
  43.1 0.7 bitcast_select_fusion.1
  43.8 0.3 reduce_window_sum.18
  44.1 0.1 select_reduce_fusion.2
  44.2 0.1 copy.50
  44.3 0.1 lt.91
  44.5 0.1 broadcast_compare_fusion
  44.6 0.2 fusion.61
  44.7 0.1 fusion.21
  44.8 178.7 %all-to-all-done = bf16[2,128,128,128]{3,2,0,1:T(8,128)(2,1)} async-done(((bf16[2,128,128,128]{3,2,0,1:T(8,128)(2,1)}), bf16[2,128,128,128]{3,2,0,1:T(8,128)(2,1)}, u32[]{:S(2)}, u32[]{:S(2)}) %all-to-all-start) | async-done | bytes 8388640 | tf_op jit(solution)/shard_map/all_to_all | solution.py:70
  223.5 4.0 fusion.58
  227.5 2.7 fusion.60
  230.2 0.2 convolution_bitcast_fusion
  230.4 0.7 fusion.3
  231.2 1.0 fusion.16
  232.2 0.2 copy-done.1
  232.4 0.9 fusion.33
  233.4 76.0 %all-reduce.2.cloned.1.call-done = f32[24,2048]{1,0:T(8,128)} async-done(((f32[24,2048]{1,0:T(8,128)}), f32[24,2048]{1,0:T(8,128)}) %all-reduce.2.cloned.1.call-update) | async-done | bytes 196624 | tf_op jit(solution)/shard_map/psum | solution.py:114
  309.4 1.1 multiply_reduce_fusion.1
  310.5 1.6 multiply_convert_fusion
  312.2 84.7 %all-gather.2.cloned.1.call-done = bf16[1536,2048]{1,0:T(8,128)(2,1)} async-done(((bf16[24,2048]{1,0:T(8,128)(2,1)}), bf16[1536,2048]{1,0:T(8,128)(2,1)}) %all-gather.2.cloned.1.call-update) | async-done | bytes 6291472 | tf_op jit(solution)/shard_map/all_gather | solution.py:122
  396.9 5.8 %fusion.62 = (f32[1536]{0:T(1024)S(1)}, f32[1536,256]{0,1:T(8,128)}) fusion(bf16[1536,2048]{1,0:T(8,128)(2,1)} %all-gather.2.cloned.1.call-done, bf16[2048,256]{1,0:T(8,128)(2,1)S(1)} %copy-done.9), kind=kOutput, calls=%fused_computation.115 | convolution fusion | flops 1611004416 | bytes 8919040 | tf_op jit(solution)/shard_map/dot_general | solution.py:121
  402.6 0.1 stack.54
  402.7 1.9 fusion.8
  404.6 0.1 stack.55
  404.7 0.1 stack.56
  404.8 0.1 stack.57
  404.9 0.7 copy.55
  405.6 7.4 %all-to-all-start.1 = ((f32[64,24,4]{1,2,0:T(4,128)}), f32[64,24,4]{1,2,0:T(4,128)S(1)}, u32[]{:S(2)}, u32[]{:S(2)}) async-start(f32[64,24,4]{1,2,0:T(4,128)} %copy.55), calls=%async_computation.1 | async-start | bytes 262144 | tf_op jit(solution)/shard_map/all_to_all | solution.py:143
  413.1 9.4 %all-to-all-done.1 = f32[64,24,4]{1,2,0:T(4,128)S(1)} async-done(((f32[64,24,4]{1,2,0:T(4,128)}), f32[64,24,4]{1,2,0:T(4,128)S(1)}, u32[]{:S(2)}, u32[]{:S(2)}) %all-to-all-start.1) | async-done | bytes 24608 | tf_op jit(solution)/shard_map/all_to_all | solution.py:143
  422.4 0.1 fusion.59
  422.7 0.2 fusion.39
  423.0 0.1 broadcast_select_fusion.1
  423.0 29.7 %psum.15 = f32[8,24,4]{1,0,2:T(8,128)S(1)} all-reduce(f32[8,24,4]{1,0,2:T(8,128)S(1)} %broadcast_select_fusion.1), channel_id=1, replica_groups=mesh['req'=64,'mdl'=8] {'mdl'}, use_global_device_ids=true, to_apply=%region_21.22 | all-reduce | flops 768 | bytes 6144 | tf_op jit(solution)/shard_map/psum | solution.py:148
  452.8 0.5 divide_subtract_fusion
  (49 shorter events, 0.6 us)
Async XLA Ops:
  7.2 4.1 copy-start
  25.0 16.8 %copy-start.10 = (s32[64]{0:T(128)S(1)}, s32[64]{0:T(128)}, u32[]{:S(2)}) copy-start(s32[64]{0:T(128)} %param.18) | copy-start | bytes 772
  25.0 19.5 %copy-start.8 = (s32[1,24]{1,0:T(1,128)S(1)}, s32[1,24]{1,0:T(1,128)}, u32[]{:S(2)}) copy-start(s32[1,24]{1,0:T(1,128)} %param.20) | copy-start | bytes 292
  25.0 19.5 %copy-start.3 = (bf16[24,256]{1,0:T(8,128)(2,1)S(1)}, bf16[24,256]{1,0:T(8,128)(2,1)}, u32[]{:S(2)}) copy-start(bf16[24,256]{1,0:T(8,128)(2,1)} %param.13) | copy-start | bytes 36868
  25.0 19.5 %copy-start.7 = (bf16[2,24,128]{2,1,0:T(8,128)(2,1)S(1)}, bf16[2,24,128]{2,1,0:T(8,128)(2,1)}, u32[]{:S(2)}) copy-start(bf16[2,24,128]{2,1,0:T(8,128)(2,1)} %param.14) | copy-start | bytes 36868
  25.0 198.5 %all-to-all-start = ((bf16[2,128,128,128]{3,2,0,1:T(8,128)(2,1)}), bf16[2,128,128,128]{3,2,0,1:T(8,128)(2,1)}, u32[]{:S(2)}, u32[]{:S(2)}) async-start(bf16[2,128,128,128]{3,2,0,1:T(8,128)(2,1)} %select_bitcast_fusion), calls=%async_computation | async-start | bytes 16777216 | tf_op jit(solution)/shard_map/all_to_all | solution.py:70
  39.2 270.2 %all-reduce.2.cloned.1.call-start = ((), (), s32[]{:S(2)}) async-start(), calls=%async_computation.2 | async-start | bytes 393216 | tf_op jit(solution)/shard_map/psum | solution.py:114
  231.1 1.2 copy-start.1
  231.1 1.2 copy-start.4
  231.1 2.2 copy-start.6
  231.1 78.3 %copy-start.2 = (bf16[24,2048]{1,0:T(8,128)(2,1)S(1)}, bf16[24,2048]{1,0:T(8,128)(2,1)}, u32[]{:S(2)}) copy-start(bf16[24,2048]{1,0:T(8,128)(2,1)} %param.21) | copy-start | bytes 294916
  231.2 165.7 %copy-start.9 = (bf16[2048,256]{1,0:T(8,128)(2,1)S(1)}, bf16[2048,256]{1,0:T(8,128)(2,1)}, u32[]{:S(2)}) copy-start(bf16[2048,256]{1,0:T(8,128)(2,1)} %param.24) | copy-start | bytes 3145732
  233.3 163.5 %all-gather.2.cloned.1.call-start = ((), (), s32[]{:S(2)}) async-start(), calls=%async_computation.3 | async-start | bytes 6389760 | tf_op jit(solution)/shard_map/all_gather | solution.py:122
  312.2 90.6 %copy-start.5 = (s32[1536]{0:T(1024)S(1)}, s32[1536]{0:T(1024)}, u32[]{:S(2)}) copy-start(s32[1536]{0:T(1024)} %param.25) | copy-start | bytes 18436
  405.6 16.8 %all-to-all-start.1 = ((f32[64,24,4]{1,2,0:T(4,128)}), f32[64,24,4]{1,2,0:T(4,128)S(1)}, u32[]{:S(2)}, u32[]{:S(2)}) async-start(f32[64,24,4]{1,2,0:T(4,128)} %copy.55), calls=%async_computation.1 | async-start | bytes 262144 | tf_op jit(solution)/shard_map/all_to_all | solution.py:143
Sparse Core Ops, SparseCore 0:
  233.4 75.9 all-reduce.1
  312.7 84.0 all-gather.1
where the time goes:
time: 461 us; the launch traced here: 460 us
  waiting for transfers between devices  349 us (76%)
  blocking collectives  29.7 us (6%)
  starting transfers between devices  21.7 us (5%)
  other arithmetic  18.1 us (4%)
  between operations  16.9 us (4%)
  local copies, waits for them, and re-layouts  14.3 us (3%)
  matrix products  10.7 us (2%)
    all_to_all x1, waiting for transfers between devices, body(): lax.all_to_all(outgoing, 'req', split_axis=1, concat_axis=1, tiled=True)  179 us
    all_gather x1, waiting for transfers between devices, body(): lax.all_gather(normed, 'req', axis=0, tiled=True)  84.7 us
    psum x1, waiting for transfers between devices, body(): lax.psum(jnp.dot(gated_out, out_weight, preferred_element_type=jnp.float3...  76 us
    psum x1, blocking collectives, body(): stats = merge_stats(lax.psum(slots, 'mdl'))  29.7 us
    all_to_all x1, starting transfers between devices, body(): lax.all_to_all(outgoing, 'req', split_axis=1, concat_axis=1, tiled=True)  14.2 us
    all_to_all x1, waiting for transfers between devices, body(): stats = lax.all_to_all(stats, 'req', 0, 0, tiled=True)  9.35 us
  transfers between devices with their start and end apart: 4, of which 4 were waited for; matrix products, arithmetic and copies ran while one was open for 1% of the time, Pallas kernels for 0%

commit v1 on v0

--- a/solution.py
+++ b/solution.py
@@ -7,6 +7,18 @@
 CAP = 2
 FLOOR_SCORE = -1e30
 NORM_EPSILON = 1e-06
+
+
+def step_on_the_tasks(page, where_dim):
+    return jnp.concatenate(
+        lax.all_to_all(
+            jnp.stack([page for _ in range(lax.axis_size("req"))]),
+            axis_name="req",
+            split_axis=0,
+            concat_axis=0,
+        ),
+        axis=where_dim,
+    )
 
 
 def merge_stats(parts):
@@ -118,11 +130,7 @@
         * lax.rsqrt(jnp.mean(stream * stream, axis=-1, keepdims=True) + NORM_EPSILON)
         * norm_gain.astype(jnp.float32)
     ).astype(jnp.bfloat16)
-    logits = jnp.dot(
-        lax.all_gather(normed, "req", axis=0, tiled=True),
-        head_weight,
-        preferred_element_type=jnp.float32,
-    )
+    logits = jnp.dot(step_on_the_tasks(normed, 0), head_weight, preferred_element_type=jnp.float32)
     vocab_width = head_weight.shape[1]
     mdl_size = lax.axis_size("mdl")
     mdl_index = lax.axis_index("mdl")

time: 461 us -> 529 us (1.15)
  waiting for transfers between devices: 349 us -> 404 us
  starting transfers between devices: 21.7 us -> 32.6 us
    all_to_all x0 -> x1, waiting for transfers between devices: none -> 139 us  [step_on_the_tasks(): lax.all_to_all(jnp.stack([page for _ in range(lax.axis_size('req'))]), ax...]
    all_gather x1 -> x0, waiting for transfers between devices: 84.7 us -> none  [body(): lax.all_gather(normed, 'req', axis=0, tiled=True)]
    all_to_all x0 -> x1, starting transfers between devices: none -> 11.2 us  [step_on_the_tasks(): lax.all_to_all(jnp.stack([page for _ in range(lax.axis_size('req'))]), ax...]
where the time goes in v1:
time: 529 us; the launch traced here: 528 us
  waiting for transfers between devices  404 us (76%)
  starting transfers between devices  32.6 us (6%)
  blocking collectives  29.1 us (6%)
  local copies, waits for them, and re-layouts  17.7 us (3%)
  other arithmetic  17.5 us (3%)
  between operations  16.9 us (3%)
  matrix products  10.7 us (2%)
    all_to_all x1, waiting for transfers between devices, body(): lax.all_to_all(outgoing, 'req', split_axis=1, concat_axis=1, tiled=True)  179 us
    all_to_all x1, waiting for transfers between devices, step_on_the_tasks(): lax.all_to_all(jnp.stack([page for _ in range(lax.axis_size('req'))]), ax...  139 us
    psum x1, waiting for transfers between devices, body(): lax.psum(jnp.dot(gated_out, out_weight, preferred_element_type=jnp.float3...  76.1 us
    psum x1, blocking collectives, body(): stats = merge_stats(lax.psum(slots, 'mdl'))  29.1 us
    all_to_all x1, starting transfers between devices, body(): lax.all_to_all(outgoing, 'req', split_axis=1, concat_axis=1, tiled=True)  14.2 us
    all_to_all x1, starting transfers between devices, step_on_the_tasks(): lax.all_to_all(jnp.stack([page for _ in range(lax.axis_size('req'))]), ax...  11.2 us
  transfers between devices with their start and end apart: 4, of which 4 were waited for; matrix products, arithmetic and copies ran while one was open for 1% of the time, Pallas kernels for 0%

profile of v1, /device:TPU:2, one launch (start us, length us, event | category | flops | bytes accessed | tf_op | source)
XLA Modules:
  0.0 528.1 jit_solution(6320056742321499790)
XLA Ops:
  7.2 0.9 select_reduce_fusion.5
  8.1 0.8 fusion.57
  8.9 0.3 reduce_window_sum.17
  9.2 0.9 select_reduce_fusion.4
  10.1 0.1 copy.49
  10.2 0.6 gather_fusion
  10.8 0.1 broadcast_select_fusion
  10.9 0.1 select_n.156
  11.1 0.1 select_n.154
  11.2 6.4 %gather_fusion.1 = bf16[128,2,128,128]{3,2,1,0:T(8,128)(2,1)} fusion(bf16[2,34,128,128]{3,2,1,0:T(8,128)(2,1)S(1)} %copy-done, s32[1024]{0:T(1024)S(1)} %pad_clamp_fusion), kind=kCustom, calls=%fused_computation.1 | custom fusion | bytes 16777728 | tf_op jit(solution)/shard_map/jit(_take)/gather | solution.py:81
  17.6 7.4 %select_bitcast_fusion = bf16[2,128,128,128]{3,2,0,1:T(8,128)(2,1)} fusion(bf16[128,2,128,128]{3,2,1,0:T(8,128)(2,1)} %gather_fusion.1, pred[128]{0:T(512)(128)(4,1)S(1)} %compare_and_fusion), kind=kLoop, calls=%fused_computation.6 | loop fusion | flops 4194304 | bytes 16777344 | tf_op jit(solution)/shard_map/jit(_take)/select_n | solution.py:81
  25.0 14.2 %all-to-all-start = ((bf16[2,128,128,128]{3,2,0,1:T(8,128)(2,1)}), bf16[2,128,128,128]{3,2,0,1:T(8,128)(2,1)}, u32[]{:S(2)}, u32[]{:S(2)}) async-start(bf16[2,128,128,128]{3,2,0,1:T(8,128)(2,1)} %select_bitcast_fusion), calls=%async_computation | async-start | bytes 16777216 | tf_op jit(solution)/shard_map/all_to_all | solution.py:82
  39.3 0.6 dynamic_slice.3
  41.8 0.6 dynamic-slice.6
  43.1 0.7 bitcast_select_fusion.1
  43.8 0.3 reduce_window_sum.18
  44.1 0.1 select_reduce_fusion.2
  44.2 0.1 copy.50
  44.3 0.1 lt.91
  44.6 0.2 fusion.61
  44.7 0.1 fusion.21
  44.8 178.7 %all-to-all-done = bf16[2,128,128,128]{3,2,0,1:T(8,128)(2,1)} async-done(((bf16[2,128,128,128]{3,2,0,1:T(8,128)(2,1)}), bf16[2,128,128,128]{3,2,0,1:T(8,128)(2,1)}, u32[]{:S(2)}, u32[]{:S(2)}) %all-to-all-start) | async-done | bytes 8388640 | tf_op jit(solution)/shard_map/all_to_all | solution.py:82
  223.5 4.0 fusion.58
  227.5 2.7 fusion.60
  230.2 0.2 convolution_bitcast_fusion
  230.4 0.7 fusion.3
  231.2 1.0 fusion.16
  232.2 0.2 copy-done.1
  232.4 0.9 fusion.33
  233.3 76.1 %all-reduce.2.cloned.1.call-done = f32[24,2048]{1,0:T(8,128)} async-done(((f32[24,2048]{1,0:T(8,128)}), f32[24,2048]{1,0:T(8,128)}) %all-reduce.2.cloned.1.call-update) | async-done | bytes 196624 | tf_op jit(solution)/shard_map/psum | solution.py:126
  309.4 1.1 multiply_reduce_fusion.1
  310.5 1.0 multiply_convert_fusion
  311.5 3.4 stack.40
  315.0 11.2 %all-to-all-start.1 = ((bf16[64,24,2048]{2,1,0:T(8,128)(2,1)}), bf16[64,24,2048]{2,1,0:T(8,128)(2,1)}, u32[]{:S(2)}, u32[]{:S(2)}) async-start(bf16[64,24,2048]{2,1,0:T(8,128)(2,1)} %stack.40), calls=%async_computation.1 | async-start | bytes 12582912 | tf_op jit(solution)/shard_map/all_to_all | solution.py:14
  326.2 139.5 %all-to-all-done.1 = bf16[64,24,2048]{2,1,0:T(8,128)(2,1)} async-done(((bf16[64,24,2048]{2,1,0:T(8,128)(2,1)}), bf16[64,24,2048]{2,1,0:T(8,128)(2,1)}, u32[]{:S(2)}, u32[]{:S(2)}) %all-to-all-start.1) | async-done | bytes 6291488 | tf_op jit(solution)/shard_map/all_to_all | solution.py:14
  465.7 5.8 %fusion.62 = (f32[1536]{0:T(1024)S(1)}, f32[1536,256]{0,1:T(8,128)}) fusion(bf16[1536,2048]{1,0:T(8,128)(2,1)} %bitcast.35, bf16[2048,256]{1,0:T(8,128)(2,1)S(1)} %copy-done.9), kind=kOutput, calls=%fused_computation.115 | convolution fusion | flops 1611004416 | bytes 8919040 | tf_op jit(solution)/shard_map/dot_general | solution.py:133
  471.5 0.1 stack.41
  471.6 1.9 fusion.8
  473.5 0.1 stack.42
  473.6 0.1 stack.43
  473.7 0.1 stack.44
  473.8 0.7 copy.55
  474.5 7.1 %all-to-all-start.2 = ((f32[64,24,4]{1,2,0:T(4,128)}), f32[64,24,4]{1,2,0:T(4,128)S(1)}, u32[]{:S(2)}, u32[]{:S(2)}) async-start(f32[64,24,4]{1,2,0:T(4,128)} %copy.55), calls=%async_computation.2 | async-start | bytes 262144 | tf_op jit(solution)/shard_map/all_to_all | solution.py:151
  481.6 9.4 %all-to-all-done.2 = f32[64,24,4]{1,2,0:T(4,128)S(1)} async-done(((f32[64,24,4]{1,2,0:T(4,128)}), f32[64,24,4]{1,2,0:T(4,128)S(1)}, u32[]{:S(2)}, u32[]{:S(2)}) %all-to-all-start.2) | async-done | bytes 24608 | tf_op jit(solution)/shard_map/all_to_all | solution.py:151
  491.0 0.1 fusion.59
  491.3 0.2 fusion.39
  491.6 29.1 %psum.15 = f32[8,24,4]{1,0,2:T(8,128)S(1)} all-reduce(f32[8,24,4]{1,0,2:T(8,128)S(1)} %broadcast_select_fusion.1), channel_id=1, replica_groups=mesh['req'=64,'mdl'=8] {'mdl'}, use_global_device_ids=true, to_apply=%region_21.22 | all-reduce | flops 768 | bytes 6144 | tf_op jit(solution)/shard_map/psum | solution.py:156
  520.7 0.5 divide_subtract_fusion
  (49 shorter events, 0.7 us)
Async XLA Ops:
  7.2 4.1 copy-start
  25.0 16.8 %copy-start.10 = (s32[64]{0:T(128)S(1)}, s32[64]{0:T(128)}, u32[]{:S(2)}) copy-start(s32[64]{0:T(128)} %param.18) | copy-start | bytes 772
  25.0 19.5 %copy-start.8 = (s32[1,24]{1,0:T(1,128)S(1)}, s32[1,24]{1,0:T(1,128)}, u32[]{:S(2)}) copy-start(s32[1,24]{1,0:T(1,128)} %param.20) | copy-start | bytes 292
  25.0 19.5 %copy-start.3 = (bf16[24,256]{1,0:T(8,128)(2,1)S(1)}, bf16[24,256]{1,0:T(8,128)(2,1)}, u32[]{:S(2)}) copy-start(bf16[24,256]{1,0:T(8,128)(2,1)} %param.13) | copy-start | bytes 36868
  25.0 19.5 %copy-start.7 = (bf16[2,24,128]{2,1,0:T(8,128)(2,1)S(1)}, bf16[2,24,128]{2,1,0:T(8,128)(2,1)}, u32[]{:S(2)}) copy-start(bf16[2,24,128]{2,1,0:T(8,128)(2,1)} %param.14) | copy-start | bytes 36868
  25.0 198.5 %all-to-all-start = ((bf16[2,128,128,128]{3,2,0,1:T(8,128)(2,1)}), bf16[2,128,128,128]{3,2,0,1:T(8,128)(2,1)}, u32[]{:S(2)}, u32[]{:S(2)}) async-start(bf16[2,128,128,128]{3,2,0,1:T(8,128)(2,1)} %select_bitcast_fusion), calls=%async_computation | async-start | bytes 16777216 | tf_op jit(solution)/shard_map/all_to_all | solution.py:82
  39.2 270.2 %all-reduce.2.cloned.1.call-start = ((), (), s32[]{:S(2)}) async-start(), calls=%async_computation.3 | async-start | bytes 393216 | tf_op jit(solution)/shard_map/psum | solution.py:126
  231.1 1.2 copy-start.1
  231.1 1.2 copy-start.4
  231.1 2.2 copy-start.6
  231.1 78.3 %copy-start.2 = (bf16[24,2048]{1,0:T(8,128)(2,1)S(1)}, bf16[24,2048]{1,0:T(8,128)(2,1)}, u32[]{:S(2)}) copy-start(bf16[24,2048]{1,0:T(8,128)(2,1)} %param.21) | copy-start | bytes 294916
  315.0 150.7 %copy-start.9 = (bf16[2048,256]{1,0:T(8,128)(2,1)S(1)}, bf16[2048,256]{1,0:T(8,128)(2,1)}, u32[]{:S(2)}) copy-start(bf16[2048,256]{1,0:T(8,128)(2,1)} %param.24) | copy-start | bytes 3145732
  315.0 150.7 %all-to-all-start.1 = ((bf16[64,24,2048]{2,1,0:T(8,128)(2,1)}), bf16[64,24,2048]{2,1,0:T(8,128)(2,1)}, u32[]{:S(2)}, u32[]{:S(2)}) async-start(bf16[64,24,2048]{2,1,0:T(8,128)(2,1)} %stack.40), calls=%async_computation.1 | async-start | bytes 12582912 | tf_op jit(solution)/shard_map/all_to_all | solution.py:14
  465.7 5.9 %copy-start.5 = (s32[1536]{0:T(1024)S(1)}, s32[1536]{0:T(1024)}, u32[]{:S(2)}) copy-start(s32[1536]{0:T(1024)} %param.25) | copy-start | bytes 18436
  474.5 16.5 %all-to-all-start.2 = ((f32[64,24,4]{1,2,0:T(4,128)}), f32[64,24,4]{1,2,0:T(4,128)S(1)}, u32[]{:S(2)}, u32[]{:S(2)}) async-start(f32[64,24,4]{1,2,0:T(4,128)} %copy.55), calls=%async_computation.2 | async-start | bytes 262144 | tf_op jit(solution)/shard_map/all_to_all | solution.py:151
Sparse Core Ops, SparseCore 0:
  233.4 75.9 all-reduce.1
